TPU v7x, 256 devices: a whole 4x4x8 slice. The times are simulated.
256 devices in a mesh: dp: 16 (over y_lo, x, core), tensor: 16 (over z, y_hi).
Axes of the slice: x: 4, y: 4 (y_hi: 2, y_lo: 2; y = y_hi * 2 + y_lo), z: 8, core: 2. Of those that a mesh axis runs over, the one named last changes fastest.
Arguments:
- gate_pre: bfloat16 [8192, 14336], P('dp', 'tensor'), may hold values from -6 to 6
- up_pre: bfloat16 [8192, 14336], P('dp', 'tensor'), may hold values from -6 to 6
- grad_out: bfloat16 [8192, 4096], P(('dp', 'tensor')), may hold values from -24 to 24
- codes: bfloat16 [14336, 4096], P('tensor'), as said below
- scales: int32 [448, 4096], P('tensor'), may hold values from 117 to 120
Outputs:
- out: bfloat16 [8192, 4096], P(('dp', 'tensor'))
- grad_gate: bfloat16 [8192, 14336], P('dp', 'tensor')
- grad_up: bfloat16 [8192, 14336], P('dp', 'tensor')
- grad_weight: bfloat16 [14336, 4096], P('tensor', 'dp')
Inputs may be any that keep to these rules, and one draw needn't show every extreme that they name: `codes`: every entry is an FP8 E4M3 normal value (sign, exponent field 4 to 9, three mantissa bits), held exactly.
All inputs are finite; a program needn't handle non-finite values.
Results may differ from a plain program's by a relative error of at most 0.022.
Values may be sent and summed in bfloat16 or wider, within the bound.
No kernel may reach another device: no remote copies, remote signals or barrier semaphores. Data moves between devices by JAX's collectives and lax.ppermute only.
A program may use at most 128 MiB of HBM per device.

v0:
```python
import jax
import jax.numpy as jnp
from jax import lax
from jax.sharding import PartitionSpec as P


def decode(codes, scales):
    factor = jnp.exp2(scales.astype(jnp.float32) - 127.0).astype(jnp.bfloat16)
    blocks = codes.reshape(scales.shape[0], 32, codes.shape[1]) * factor[:, None, :]
    return blocks.reshape(codes.shape)


def weight_gradient(hidden, cotangent):
    partial_grad = lax.dot_general(
        hidden, cotangent, (((0,), (0,)), ((), ())), preferred_element_type=jnp.float32
    )
    return lax.psum_scatter(
        partial_grad.astype(jnp.bfloat16), "dp", scatter_dimension=1, tiled=True
    )


def per_device(gate_pre, up_pre, grad_out, codes, scales):
    weight = decode(codes, scales)
    gate_value = gate_pre.astype(jnp.float32)
    up_value = up_pre.astype(jnp.float32)
    sigmoid_gate = jax.nn.sigmoid(gate_value)
    hidden = (gate_value * sigmoid_gate * up_value).astype(jnp.bfloat16)
    out = lax.psum_scatter(
        jnp.dot(hidden, weight, preferred_element_type=jnp.float32).astype(jnp.bfloat16),
        "tensor",
        scatter_dimension=0,
        tiled=True,
    )
    cotangent = lax.all_gather(grad_out, "tensor", axis=0, tiled=True)
    grad_hidden = lax.dot_general(
        cotangent, weight, (((1,), (1,)), ((), ())), preferred_element_type=jnp.float32
    )
    grad_weight = weight_gradient(hidden, cotangent)
    grad_gate = (
        grad_hidden * up_value * sigmoid_gate * (1.0 + gate_value * (1.0 - sigmoid_gate))
    ).astype(jnp.bfloat16)
    grad_up = (grad_hidden * gate_value * sigmoid_gate).astype(jnp.bfloat16)
    return (out, grad_gate, grad_up, grad_weight)


def solution(mesh):
    in_specs = (
        P("dp", "tensor"),
        P("dp", "tensor"),
        P(("dp", "tensor"), None),
        P("tensor", None),
        P("tensor", None),
    )
    out_specs = (P(("dp", "tensor"), None), P("dp", "tensor"), P("dp", "tensor"), P("tensor", "dp"))
    return jax.shard_map(
        per_device, mesh=mesh, in_specs=in_specs, out_specs=out_specs, check_vma=False
    )
```

profile of v0, /device:TPU:16, one launch (start us, length us, event | category | flops | bytes accessed | tf_op | source)
XLA Modules:
  0.0 412.0 jit_solution(5260447283789857836)
XLA Ops:
  7.2 0.0 copy-start.1
  7.2 0.0 all-gather.2.cloned.1.call-start
  7.2 0.7 all-gather.2.cloned.1.call-update
  7.9 0.0 copy-start.4
  7.9 0.0 reduce-scatter.3.cloned.1.call-start
  8.0 2.3 copy.10
  10.2 0.0 copy-done.1
  10.2 1.3 copy.9
  11.5 0.0 copy-done.4
  11.5 0.1 exponential_convert_fusion
  11.6 3.7 bitcast_multiply_fusion
  15.3 0.0 copy-start
  15.3 2.9 copy-done
  18.2 8.0 %convolution_convert_fusion.1 = bf16[512,4096]{1,0:T(8,128)(2,1)} fusion(bf16[896,4096]{1,0:T(8,128)(2,1)S(1)} %bitcast_multiply_fusion, bf16[512,896]{0,1:T(8,128)(2,1)} %copy.10, bf16[512,896]{0,1:T(8,128)(2,1)} %copy.9), kind=kOutput, calls=%fused_computation.2 | convolution fusion | flops 3763863552 | bytes 13369344 | tf_op jit(solution)/shard_map/dot_general | solution.py:29
  26.3 0.0 copy-start.2
  26.3 0.0 copy-start.3
  26.3 0.0 reduce-scatter.3.cloned.1.call-update
  26.3 0.0 reduce-scatter.5.cloned.1.call-start
  26.3 84.5 %all-gather.2.cloned.1.call-done = bf16[512,4096]{1,0:T(8,128)(2,1)} async-done(((bf16[32,4096]{1,0:T(8,128)(2,1)}), bf16[512,4096]{1,0:T(8,128)(2,1)}) %all-gather.2.cloned.1.call-update) | async-done | bytes 4194320 | tf_op jit(solution)/shard_map/all_gather | solution.py:34
  110.9 0.0 copy-done.2
  110.9 0.0 copy-done.3
  110.9 8.4 %convolution_convert_fusion = bf16[896,4096]{1,0:T(8,128)(2,1)} fusion(bf16[512,4096]{1,0:T(8,128)(2,1)} %all-gather.2.cloned.1.call-done, bf16[512,896]{0,1:T(8,128)(2,1)S(1)} %copy-done.2, bf16[512,896]{0,1:T(8,128)(2,1)S(1)} %copy-done.3), kind=kOutput, calls=%fused_computation.1 | convolution fusion | flops 3765436416 | bytes 13369344 | tf_op jit(solution)/shard_map/dot_general | solution.py:14
  119.3 0.0 reduce-scatter.5.cloned.1.call-update
  119.3 9.8 %fusion.9 = (bf16[512,896]{0,1:T(8,128)(2,1)S(1)}, bf16[512,896]{0,1:T(8,128)(2,1)}) fusion(bf16[512,896]{0,1:T(8,128)(2,1)S(1)} %copy-done.3, bf16[512,896]{0,1:T(8,128)(2,1)S(1)} %copy-done.2, bf16[896,4096]{1,0:T(8,128)(2,1)} %copy-done, bf16[512,4096]{1,0:T(8,128)(2,1)} %all-gather.2.cloned.1.call-done), kind=kOutput, calls=%fused_computation.18 | convolution fusion | flops 3764977664 | bytes 15204352 | tf_op jit(solution)/shard_map/dot_general | solution.py:35
  129.1 2.2 copy.11
  131.3 1.3 copy.12
  132.6 194.3 %reduce-scatter.3.cloned.1.call-done = bf16[32,4096]{1,0:T(8,128)(2,1)} async-done(((bf16[512,4096]{1,0:T(8,128)(2,1)}), bf16[32,4096]{1,0:T(8,128)(2,1)}) %reduce-scatter.3.cloned.1.call-update) | async-done | bytes 262160 | tf_op jit(solution)/shard_map/reduce_scatter | solution.py:28
  326.9 78.5 %reduce-scatter.5.cloned.1.call-done = bf16[896,256]{1,0:T(8,128)(2,1)} async-done(((bf16[896,4096]{1,0:T(8,128)(2,1)}), bf16[896,256]{1,0:T(8,128)(2,1)}) %reduce-scatter.5.cloned.1.call-update) | async-done | bytes 458768 | tf_op jit(solution)/shard_map/reduce_scatter | solution.py:17
Async XLA Ops:
  7.2 3.1 copy-start.1
  7.2 103.7 %all-gather.2.cloned.1.call-start = ((), (), s32[]{:S(2)}) async-start(), calls=%async_computation.3 | async-start | bytes 4456448 | tf_op jit(solution)/shard_map/all_gather | solution.py:34
  7.9 3.6 copy-start.4
  7.9 319.0 %reduce-scatter.3.cloned.1.call-start = ((), (), s32[]{:S(2)}) async-start(), calls=%async_computation.2 | async-start | bytes 4456448 | tf_op jit(solution)/shard_map/reduce_scatter | solution.py:28
  15.3 2.9 copy-start
  26.3 84.6 %copy-start.2 = (bf16[512,896]{0,1:T(8,128)(2,1)S(1)}, bf16[512,896]{0,1:T(8,128)(2,1)}, u32[]{:S(2)}) copy-start(bf16[512,896]{0,1:T(8,128)(2,1)} %copy.10) | copy-start | bytes 2752516
  26.3 84.6 %copy-start.3 = (bf16[512,896]{0,1:T(8,128)(2,1)S(1)}, bf16[512,896]{0,1:T(8,128)(2,1)}, u32[]{:S(2)}) copy-start(bf16[512,896]{0,1:T(8,128)(2,1)} %copy.9) | copy-start | bytes 2752516
  26.3 379.1 %reduce-scatter.5.cloned.1.call-start = ((), (), s32[]{:S(2)}) async-start(), calls=%async_computation.4 | async-start | bytes 7798784 | tf_op jit(solution)/shard_map/reduce_scatter | solution.py:17
Sparse Core Ops, SparseCore 0:
  10.6 100.2 all-gather.1
  115.5 211.3 reduce-scatter.2
  330.0 75.3 reduce-scatter.4
where the time goes:
time: 412 us
  waiting for transfers between devices  358 us (87%)
  matrix products  26.2 us (6%)
  between operations  13.8 us (3%)
  local copies, waits for them, and re-layouts  9.97 us (2%)
    reduce_scatter x1, waiting for transfers between devices, per_device(): lax.psum_scatter(jnp.dot(hidden, weight, preferred_element_type=jnp.float...  194 us
    all_gather x1, waiting for transfers between devices, per_device(): cotangent = lax.all_gather(grad_out, 'tensor', axis=0, tiled=True)  84.5 us
    reduce_scatter x1, waiting for transfers between devices, weight_gradient(): lax.psum_scatter(partial_grad.astype(jnp.bfloat16), 'dp', scatter_dimensi...  78.5 us
    unnamed x14, local copies, waits for them, and re-layouts  9.97 us
    dot_general x1, matrix products, per_device(): lax.dot_general(cotangent, weight, (((1,), (1,)), ((), ())), preferred_el...  9.8 us
    dot_general x1, matrix products, weight_gradient(): lax.dot_general(hidden, cotangent, (((0,), (0,)), ((), ())), preferred_el...  8.41 us
  transfers between devices with their start and end apart: 3, of which 3 were waited for; matrix products, arithmetic and copies ran while one was open for 9% of the time, Pallas kernels for 0%

commit v1 on v0

--- a/solution.py
+++ b/solution.py
@@ -31,7 +31,14 @@
         scatter_dimension=0,
         tiled=True,
     )
-    cotangent = lax.all_gather(grad_out, "tensor", axis=0, tiled=True)
+
+    def pair_regions(piece_in, dim_i):
+        even = lax.all_to_all(
+            jnp.stack([piece_in] * lax.axis_size("tensor"), axis=0), "tensor", 0, 0
+        )
+        return jnp.concatenate(even, axis=dim_i)
+
+    cotangent = pair_regions(grad_out, 0)
     grad_hidden = lax.dot_general(
         cotangent, weight, (((1,), (1,)), ((), ())), preferred_element_type=jnp.float32
     )

time: 412 us -> 375 us (0.910)
  waiting for transfers between devices: 358 us -> 306 us
  starting transfers between devices: 0.12 us -> 11.7 us
    all_to_all x0 -> x1, waiting for transfers between devices: none -> 90.6 us  [pair_regions(): lax.all_to_all(jnp.stack([piece_in] * lax.axis_size('tensor'), axis=0), '...]
    all_gather x1 -> x0, waiting for transfers between devices: 84.5 us -> none  [per_device(): cotangent = lax.all_gather(grad_out, 'tensor', axis=0, tiled=True)]
    reduce_scatter x1, waiting for transfers between devices: 194 us -> 137 us  [per_device(): lax.psum_scatter(jnp.dot(hidden, weight, preferred_element_type=jnp.float...]
    all_to_all x0 -> x1, starting transfers between devices: none -> 11.6 us  [pair_regions(): lax.all_to_all(jnp.stack([piece_in] * lax.axis_size('tensor'), axis=0), '...]
    unnamed x14 -> x16, local copies, waits for them, and re-layouts: 9.97 us -> 9 us
  transfers between devices with their start and end apart: 3 -> 3, of which waited for: 3 -> 3; matrix products, arithmetic and copies ran while one was open for 9% -> 10% of each run, Pallas kernels for 0% -> 0%
where the time goes in v1:
time: 375 us; the launch traced here: 374 us
  waiting for transfers between devices  306 us (82%)
  matrix products  26.3 us (7%)
  between operations  14.1 us (4%)
  local copies, waits for them, and re-layouts  12.5 us (3%)
  starting transfers between devices  11.7 us (3%)
  other arithmetic  3.78 us (1%)
    reduce_scatter x1, waiting for transfers between devices, per_device(): lax.psum_scatter(jnp.dot(hidden, weight, preferred_element_type=jnp.float...  137 us
    all_to_all x1, waiting for transfers between devices, pair_regions(): lax.all_to_all(jnp.stack([piece_in] * lax.axis_size('tensor'), axis=0), '...  90.6 us
    reduce_scatter x1, waiting for transfers between devices, weight_gradient(): lax.psum_scatter(partial_grad.astype(jnp.bfloat16), 'dp', scatter_dimensi...  78.5 us
    all_to_all x1, starting transfers between devices, pair_regions(): lax.all_to_all(jnp.stack([piece_in] * lax.axis_size('tensor'), axis=0), '...  11.6 us
    dot_general x1, matrix products, per_device(): lax.dot_general(cotangent, weight, (((1,), (1,)), ((), ())), preferred_el...  9.88 us
    unnamed x16, local copies, waits for them, and re-layouts  9 us
    dot_general x1, matrix products, weight_gradient(): lax.dot_general(hidden, cotangent, (((0,), (0,)), ((), ())), preferred_el...  8.45 us
    dot_general x1, matrix products, per_device(): jnp.dot(hidden, weight, preferred_element_type=jnp.float32)  8.01 us
  transfers between devices with their start and end apart: 3, of which 3 were waited for; matrix products, arithmetic and copies ran while one was open for 10% of the time, Pallas kernels for 0%

profile of v1, /device:TPU:16, one launch (start us, length us, event | category | flops | bytes accessed | tf_op | source)
XLA Modules:
  0.0 374.4 jit_solution(15893544604850621305)
XLA Ops:
  7.2 3.5 stack.2
  10.7 0.0 copy-start.5
  10.7 0.0 copy-start.1
  10.7 11.6 %all-to-all-start = ((bf16[16,32,4096]{2,1,0:T(8,128)(2,1)}), bf16[16,32,4096]{2,1,0:T(8,128)(2,1)}, u32[]{:S(2)}, u32[]{:S(2)}) async-start(bf16[16,32,4096]{2,1,0:T(8,128)(2,1)} %stack.2), calls=%async_computation.1 | async-start | bytes 8388608 | tf_op jit(solution)/shard_map/all_to_all | solution.py:36
  22.3 0.0 copy-start.2
  22.3 0.0 reduce-scatter.3.cloned.1.call-start
  22.3 0.0 copy-done.5
  22.3 0.1 exponential_convert_fusion
  22.5 0.0 copy-done.1
  22.5 1.3 copy.10
  23.8 0.0 copy-done.2
  23.8 1.3 copy.9
  25.0 3.7 bitcast_multiply_fusion
  28.7 0.0 copy-start
  28.7 2.9 copy-done
  31.7 8.0 %convolution_convert_fusion.1 = bf16[512,4096]{1,0:T(8,128)(2,1)} fusion(bf16[896,4096]{1,0:T(8,128)(2,1)S(1)} %bitcast_multiply_fusion, bf16[512,896]{0,1:T(8,128)(2,1)} %copy.10, bf16[512,896]{0,1:T(8,128)(2,1)} %copy.9), kind=kOutput, calls=%fused_computation.2 | convolution fusion | flops 3763863552 | bytes 13369344 | tf_op jit(solution)/shard_map/dot_general | solution.py:29
  39.7 0.0 copy-start.3
  39.7 0.0 copy-start.4
  39.7 0.0 reduce-scatter.3.cloned.1.call-update
  39.7 0.0 reduce-scatter.5.cloned.1.call-start
  39.7 90.6 %all-to-all-done = bf16[16,32,4096]{2,1,0:T(8,128)(2,1)} async-done(((bf16[16,32,4096]{2,1,0:T(8,128)(2,1)}), bf16[16,32,4096]{2,1,0:T(8,128)(2,1)}, u32[]{:S(2)}, u32[]{:S(2)}) %all-to-all-start) | async-done | bytes 4194336 | tf_op jit(solution)/shard_map/all_to_all | solution.py:36
  130.4 0.0 copy-done.3
  130.4 0.0 copy-done.4
  130.4 8.4 %convolution_convert_fusion = bf16[896,4096]{1,0:T(8,128)(2,1)} fusion(bf16[512,4096]{1,0:T(8,128)(2,1)} %bitcast.1, bf16[512,896]{0,1:T(8,128)(2,1)S(1)} %copy-done.3, bf16[512,896]{0,1:T(8,128)(2,1)S(1)} %copy-done.4), kind=kOutput, calls=%fused_computation.1 | convolution fusion | flops 3765436416 | bytes 13369344 | tf_op jit(solution)/shard_map/dot_general | solution.py:14
  138.8 0.0 reduce-scatter.5.cloned.1.call-update
  138.8 9.9 %fusion.9 = (bf16[512,896]{0,1:T(8,128)(2,1)S(1)}, bf16[512,896]{0,1:T(8,128)(2,1)}) fusion(bf16[512,896]{0,1:T(8,128)(2,1)S(1)} %copy-done.4, bf16[512,896]{0,1:T(8,128)(2,1)S(1)} %copy-done.3, bf16[896,4096]{1,0:T(8,128)(2,1)} %copy-done, bf16[512,4096]{1,0:T(8,128)(2,1)} %bitcast.1), kind=kOutput, calls=%fused_computation.18 | convolution fusion | flops 3764977664 | bytes 15204352 | tf_op jit(solution)/shard_map/dot_general | solution.py:42
  148.7 2.2 copy.11
  150.9 1.3 copy.12
  152.2 136.8 %reduce-scatter.3.cloned.1.call-done = bf16[32,4096]{1,0:T(8,128)(2,1)} async-done(((bf16[512,4096]{1,0:T(8,128)(2,1)}), bf16[32,4096]{1,0:T(8,128)(2,1)}) %reduce-scatter.3.cloned.1.call-update) | async-done | bytes 262160 | tf_op jit(solution)/shard_map/reduce_scatter | solution.py:28
  289.1 78.5 %reduce-scatter.5.cloned.1.call-done = bf16[896,256]{1,0:T(8,128)(2,1)} async-done(((bf16[896,4096]{1,0:T(8,128)(2,1)}), bf16[896,256]{1,0:T(8,128)(2,1)}) %reduce-scatter.5.cloned.1.call-update) | async-done | bytes 458768 | tf_op jit(solution)/shard_map/reduce_scatter | solution.py:17
Async XLA Ops:
  10.7 11.6 %copy-start.5 = (s32[28,4096]{1,0:T(8,128)S(1)}, s32[28,4096]{1,0:T(8,128)}, u32[]{:S(2)}) copy-start(s32[28,4096]{1,0:T(8,128)} %param.9) | copy-start | bytes 1376260
  10.7 11.8 %copy-start.1 = (bf16[512,896]{1,0:T(8,128)(2,1)S(1)}, bf16[512,896]{1,0:T(8,128)(2,1)}, u32[]{:S(2)}) copy-start(bf16[512,896]{1,0:T(8,128)(2,1)} %param.6) | copy-start | bytes 2752516
  10.7 119.7 %all-to-all-start = ((bf16[16,32,4096]{2,1,0:T(8,128)(2,1)}), bf16[16,32,4096]{2,1,0:T(8,128)(2,1)}, u32[]{:S(2)}, u32[]{:S(2)}) async-start(bf16[16,32,4096]{2,1,0:T(8,128)(2,1)} %stack.2), calls=%async_computation.1 | async-start | bytes 8388608 | tf_op jit(solution)/shard_map/all_to_all | solution.py:36
  22.3 1.5 copy-start.2
  22.3 266.8 %reduce-scatter.3.cloned.1.call-start = ((), (), s32[]{:S(2)}) async-start(), calls=%async_computation.3 | async-start | bytes 4456448 | tf_op jit(solution)/shard_map/reduce_scatter | solution.py:28
  28.7 2.9 copy-start
  39.7 90.7 %copy-start.3 = (bf16[512,896]{0,1:T(8,128)(2,1)S(1)}, bf16[512,896]{0,1:T(8,128)(2,1)}, u32[]{:S(2)}) copy-start(bf16[512,896]{0,1:T(8,128)(2,1)} %copy.10) | copy-start | bytes 2752516
  39.7 90.7 %copy-start.4 = (bf16[512,896]{0,1:T(8,128)(2,1)S(1)}, bf16[512,896]{0,1:T(8,128)(2,1)}, u32[]{:S(2)}) copy-start(bf16[512,896]{0,1:T(8,128)(2,1)} %copy.9) | copy-start | bytes 2752516
  39.7 327.8 %reduce-scatter.5.cloned.1.call-start = ((), (), s32[]{:S(2)}) async-start(), calls=%async_computation.4 | async-start | bytes 7798784 | tf_op jit(solution)/shard_map/reduce_scatter | solution.py:17
Sparse Core Ops, SparseCore 0:
  39.8 249.1 reduce-scatter.2
  292.2 75.2 reduce-scatter.4
